TPU v7x, 128 devices: a whole 4x4x4 slice. The times are simulated.
128 devices in a mesh: grp: 8 (over z, core), dev: 16 (over y, x).
Axes of the slice: x: 4, y: 4, z: 4, core: 2. Of those that a mesh axis runs over, the one named last changes fastest.
Arguments:
- positions: float32 [3, 131072], P(None, ('grp', 'dev')), may hold values from -3 to 3
- velocities: float32 [3, 131072], P(None, ('grp', 'dev')), may hold values from -5 to 5
- accelerations: float32 [3, 131072], P(None, ('grp', 'dev')), may hold values from -3 to 3
- jerks: float32 [3, 131072], P(None, ('grp', 'dev')), may hold values from -3 to 3
- levels: int32 [131072], P(('grp', 'dev')), may hold values from 0 to 5
- counts: int32 [2, 128], replicated, may hold values from 1 to 256, 16384 in all within a row
- active_rows: int32 [2, 32768], P(None, ('grp', 'dev')), may hold values from 0 to 1023, as said below
Outputs:
- new_positions: float32 [3, 131072], P(None, ('grp', 'dev'))
- new_velocities: float32 [3, 131072], P(None, ('grp', 'dev'))
- new_accelerations: float32 [3, 131072], P(None, ('grp', 'dev'))
- new_jerks: float32 [3, 131072], P(None, ('grp', 'dev'))
Inputs may be any that keep to these rules, and one draw needn't show every extreme that they name: In each step the 128 counts sum to exactly 16384 and the largest of them is exactly 256. `active_rows`: for each step and device, the 256 entries of the device's slots are distinct indices of that device's own stars; only the first counts of them are live.
All inputs are finite; a program needn't handle non-finite values.
Results may differ from a plain program's by a relative error of at most 0.00022.
Values sent between devices are 32-bit elements; how exact they have to be, the bound alone decides.
No kernel may reach another device: no remote copies, remote signals or barrier semaphores. Data moves between devices by JAX's collectives and lax.ppermute only.
A program may use at most 128 MiB of HBM per device.

v0:
```python
import math

import jax
import jax.numpy as jnp
from jax import lax
from jax.experimental import pallas as pl
from jax.experimental.pallas import tpu as pltpu
from jax.sharding import PartitionSpec as P

tick_length = 1.0 / 128.0


LANES = 128
SUB = 8


def _pair_terms_kernel(cnt_ref, tgt_ref, src_ref, out_ref, *, soft_sq, mass, n_chunks, n_owner, slot_cap):
    out_ref[...] = jnp.zeros(out_ref.shape, jnp.float32)

    def one_group(base):
        tile = tgt_ref[pl.ds(base, 2 * SUB), :]
        halves = []
        for h in range(2):
            part = tile[h * SUB:(h + 1) * SUB, :]
            halves.append([jnp.broadcast_to(part[:, k:k + 1], (SUB, LANES)) for k in range(6)])

        def chunk(c, accs):
            off = pl.multiple_of(c * LANES, LANES)
            s = [src_ref[k, :, pl.ds(off, LANES)] for k in range(6)]
            new = []
            for h in range(2):
                t = halves[h]
                a = accs[6 * h:6 * h + 6]
                dx = s[0] - t[0]
                dy = s[1] - t[1]
                dz = s[2] - t[2]
                ux = s[3] - t[3]
                uy = s[4] - t[4]
                uz = s[5] - t[5]
                r2 = dx * dx + dy * dy + dz * dz + soft_sq
                inv = lax.rsqrt(r2)
                inv2 = inv * inv
                w = inv * inv2
                al = 3.0 * (dx * ux + dy * uy + dz * uz) * inv2
                new += [
                    a[0] + w * dx,
                    a[1] + w * dy,
                    a[2] + w * dz,
                    a[3] + w * (ux - al * dx),
                    a[4] + w * (uy - al * dy),
                    a[5] + w * (uz - al * dz),
                ]
            return tuple(new)

        zero = jnp.zeros((SUB, LANES), jnp.float32)
        accs = lax.fori_loop(0, n_chunks, chunk, (zero,) * 12, unroll=4)
        for h in range(2):
            for k in range(6):
                total = jnp.sum(accs[6 * h + k], axis=1, keepdims=True) * mass
                out_ref[pl.ds(base + h * SUB, SUB), pl.ds(k, 1)] = total

    def one_owner(o, carry):
        n_groups = (jnp.clip(cnt_ref[o], 0, slot_cap) + 2 * SUB - 1) // (2 * SUB)

        def body(gi, c):
            one_group(pl.multiple_of(o * slot_cap + gi * (2 * SUB), 2 * SUB))
            return c

        return lax.fori_loop(0, n_groups, body, carry)

    lax.fori_loop(0, n_owner, one_owner, 0)


def pair_terms(col_counts, tgt, src, mass, soft_sq, interpret=False):
    cap = tgt.shape[0]
    n_owner = col_counts.shape[0]
    n_src = src.shape[1]
    src_b = jnp.broadcast_to(src[:, None, :], (6, SUB, n_src))
    kernel = lambda *refs: _pair_terms_kernel(
        *refs, soft_sq=soft_sq, mass=mass, n_chunks=n_src // LANES, n_owner=n_owner, slot_cap=cap // n_owner
    )
    return pl.pallas_call(
        kernel,
        out_shape=jax.ShapeDtypeStruct((cap, 8), jnp.float32),
        in_specs=[
            pl.BlockSpec(memory_space=pltpu.SMEM),
            pl.BlockSpec(memory_space=pltpu.VMEM),
            pl.BlockSpec(memory_space=pltpu.VMEM),
        ],
        out_specs=pl.BlockSpec(memory_space=pltpu.VMEM),
        interpret=interpret,
    )(col_counts.astype(jnp.int32), tgt, src_b)


def pair_block(targets, src_pos, src_vel, mass, soft_sq):
    gap_x = src_pos[0][None, :] - targets[0][:, None]
    gap_y = src_pos[1][None, :] - targets[1][:, None]
    gap_z = src_pos[2][None, :] - targets[2][:, None]
    drift_x = src_vel[0][None, :] - targets[3][:, None]
    drift_y = src_vel[1][None, :] - targets[4][:, None]
    drift_z = src_vel[2][None, :] - targets[5][:, None]
    squared = gap_x * gap_x + gap_y * gap_y + gap_z * gap_z + soft_sq
    inverse = lax.rsqrt(squared)
    weight = mass * inverse * inverse * inverse
    along = 3.0 * (gap_x * drift_x + gap_y * drift_y + gap_z * drift_z) * inverse * inverse
    return jnp.stack(
        [
            jnp.sum(weight * gap_x, axis=1),
            jnp.sum(weight * gap_y, axis=1),
            jnp.sum(weight * gap_z, axis=1),
            jnp.sum(weight * (drift_x - along * gap_x), axis=1),
            jnp.sum(weight * (drift_y - along * gap_y), axis=1),
            jnp.sum(weight * (drift_z - along * gap_z), axis=1),
        ]
    )


def block_terms(packed, src_pos, src_vel, mass, soft_sq):
    width, total = packed.shape
    block = math.gcd(total, 2048)
    grouped = packed.reshape(width, total // block, block).transpose(1, 0, 2)
    result = lax.map(lambda targets: pair_block(targets, src_pos, src_vel, mass, soft_sq), grouped)
    return result.transpose(1, 0, 2).reshape(width, total)


def predict(positions, velocities, accelerations, jerks, elapsed):
    span = elapsed[None, :]
    pred_pos = (
        positions
        + span * velocities
        + 0.5 * span * span * accelerations
        + span * span * span / 6.0 * jerks
    )
    pred_vel = velocities + span * accelerations + 0.5 * span * span * jerks
    return (pred_pos, pred_vel)


def correct(old_pos, old_vel, old_acc, old_jerk, force, jerk_new, span):
    span = span[None, :]
    new_vel = old_vel + 0.5 * span * (old_acc + force) + span * span / 12.0 * (old_jerk - jerk_new)
    new_pos = old_pos + 0.5 * span * (old_vel + new_vel) + span * span / 12.0 * (old_acc - force)
    return (new_pos, new_vel)


def shards(positions, velocities, accelerations, jerks, levels, counts, active_rows):
    n_grp = lax.axis_size("grp")
    n_dev = lax.axis_size("dev")
    g_idx = lax.axis_index("grp")
    d_idx = lax.axis_index("dev")
    devices_all = n_grp * n_dev
    star_dev = positions.shape[1]
    slot_cap = active_rows.shape[1]
    stars_all = star_dev * devices_all
    mass = 1.0 / stars_all
    soft_sq = 0.0004 * (131072.0 / stars_all) ** (2.0 / 3.0)
    col_cap = n_grp * slot_cap
    last_time = -(jnp.left_shift(jnp.int32(1), levels) - 1).astype(jnp.float32) * tick_length
    for step in range(active_rows.shape[0]):
        now = (step + 1) * tick_length
        pred_pos, pred_vel = predict(positions, velocities, accelerations, jerks, now - last_time)
        rows = active_rows[step]
        targets = jnp.concatenate([pred_pos[:, rows], pred_vel[:, rows]], axis=0)
        col_counts = counts[step].reshape(n_grp, n_dev)[:, d_idx]
        col_targets = lax.all_gather(targets, "grp", axis=1, tiled=True)
        padded = jnp.concatenate([col_targets, jnp.zeros((2, col_cap), jnp.float32)], axis=0)
        src = lax.all_gather(jnp.concatenate([pred_pos, pred_vel], axis=0), "dev", axis=1, tiled=True)
        partial = pair_terms(col_counts, padded.T, src, mass, soft_sq)
        totals = lax.psum(partial[:, :6].T, "grp")
        own = lax.dynamic_slice_in_dim(totals, g_idx * slot_cap, slot_cap, 1)
        own_count = col_counts[g_idx]
        span = now - last_time[rows]
        new_pos, new_vel = correct(
            positions[:, rows],
            velocities[:, rows],
            accelerations[:, rows],
            jerks[:, rows],
            own[:3],
            own[3:],
            span,
        )
        live = jnp.arange(slot_cap, dtype=jnp.int32) < own_count
        target = jnp.where(live, rows, star_dev)
        positions = positions.at[:, target].set(new_pos, mode="drop")
        velocities = velocities.at[:, target].set(new_vel, mode="drop")
        accelerations = accelerations.at[:, target].set(own[:3], mode="drop")
        jerks = jerks.at[:, target].set(own[3:], mode="drop")
        last_time = last_time.at[target].set(now, mode="drop")
    return (positions, velocities, accelerations, jerks)


def solution(mesh):
    placed = (
        P(None, ("grp", "dev")),
        P(None, ("grp", "dev")),
        P(None, ("grp", "dev")),
        P(None, ("grp", "dev")),
        P(("grp", "dev")),
        P(),
        P(None, ("grp", "dev")),
    )
    return jax.shard_map(
        shards,
        mesh=mesh,
        in_specs=placed,
        out_specs=(
            P(None, ("grp", "dev")),
            P(None, ("grp", "dev")),
            P(None, ("grp", "dev")),
            P(None, ("grp", "dev")),
        ),
        check_vma=False,
    )
```

profile of v0, /device:TPU:28, one launch (start us, length us, event | category | flops | bytes accessed | tf_op | source)
XLA Modules:
  0.0 548.5 jit_solution(10305801790849909356)
XLA Ops:
  0.6 0.8 slice_reduce_fusion
  2.8 2.6 compare_select_fusion
  5.4 0.7 negate_multiply_fusion
  6.1 0.8 multiply_add_fusion.3
  7.1 0.7 gather_fusion.3
  8.1 0.7 gather_fusion.4
  8.9 15.0 %all_gather.12 = f32[6,2048]{0,1:T(8,128)S(1)} all-gather(f32[6,256]{0,1:T(8,128)S(1)} %pad_maximum_fusion), channel_id=1, replica_groups=mesh['grp'=8,'dev'=16] {'grp'}, dimensions={1}, use_global_device_ids=true | all-gather | bytes 55296 | tf_op jit(solution)/shard_map/all_gather | solution.py:164
  23.9 1.1 pad_bitcast_fusion.1.refs_1_
  25.0 22.1 %all_gather.13 = f32[6,16384]{1,0:T(8,128)S(1)} all-gather(f32[6,1024]{1,0:T(8,128)S(1)} %pad_maximum_fusion.2), channel_id=1, replica_groups=mesh['grp'=8,'dev'=16] {'dev'}, dimensions={1}, use_global_device_ids=true | all-gather | bytes 417792 | tf_op jit(solution)/shard_map/all_gather | solution.py:166
  47.1 1.9 broadcast_in_dim.9.refs_2_
  48.9 0.7 dynamic-slice_reduce_fusion.1.refs_0_
  49.6 125.0 %shard_map.102 = f32[2048,8]{1,0:T(8,128)} custom-call(s32[8]{0:T(128)} %dynamic-slice_reduce_fusion.1.refs_0_, f32[2048,8]{1,0:T(8,128)} %pad_bitcast_fusion.1.refs_1_, f32[6,8,16384]{2,1,0:T(8,128)} %broadcast_in_dim.9.refs_2_), custom_call_target="tpu_custom_call" | custom-call | tf_op jit(solution)/shard_map/pallas_call | solution.py:82
  174.7 1.3 slice_bitcast_fusion.1
  176.0 50.1 %psum.14 = f32[6,2048]{0,1:T(8,128)S(1)} all-reduce(f32[6,2048]{0,1:T(8,128)S(1)} %slice_bitcast_fusion.1), channel_id=1, replica_groups=mesh['grp'=8,'dev'=16] {'grp'}, use_global_device_ids=true, to_apply=%region_0.0 | all-reduce | flops 12288 | bytes 98304 | tf_op jit(solution)/shard_map/psum | solution.py:168
  226.1 1.4 gather_fusion
  227.7 0.7 gather_fusion.1
  228.7 0.7 gather_fusion.2
  229.7 0.7 gather_fusion.5
  230.6 1.4 scatter_custom_fusion.2
  232.0 0.8 copy.136
  232.8 0.9 copy.133
  233.7 2.1 scatter_custom_fusion
  236.1 1.6 scatter_custom_fusion.4
  237.9 1.5 scatter_custom_fusion.3
  239.6 1.7 scatter_fusion
  241.3 62.1 %all_gather.15 = f32[6,16384]{1,0:T(8,128)S(1)} all-gather(f32[6,1024]{1,0:T(8,128)S(1)} %pad_maximum_fusion.3), channel_id=1, replica_groups=mesh['grp'=8,'dev'=16] {'dev'}, dimensions={1}, use_global_device_ids=true | all-gather | bytes 417792 | tf_op jit(solution)/shard_map/all_gather | solution.py:166
  303.5 1.9 broadcast_in_dim.10.refs_2_
  305.6 0.7 gather_fusion.9
  306.6 0.7 gather_fusion.10
  307.4 13.9 %all_gather.14 = f32[6,2048]{0,1:T(8,128)S(1)} all-gather(f32[6,256]{0,1:T(8,128)S(1)} %pad_maximum_fusion.1), channel_id=1, replica_groups=mesh['grp'=8,'dev'=16] {'grp'}, dimensions={1}, use_global_device_ids=true | all-gather | bytes 55296 | tf_op jit(solution)/shard_map/all_gather | solution.py:164
  321.3 1.1 pad_bitcast_fusion.refs_1_
  322.4 0.7 dynamic-slice_reduce_fusion.refs_0_
  323.1 157.6 %shard_map.103 = f32[2048,8]{1,0:T(8,128)} custom-call(s32[8]{0:T(128)} %dynamic-slice_reduce_fusion.refs_0_, f32[2048,8]{1,0:T(8,128)} %pad_bitcast_fusion.refs_1_, f32[6,8,16384]{2,1,0:T(8,128)} %broadcast_in_dim.10.refs_2_), custom_call_target="tpu_custom_call" | custom-call | tf_op jit(solution)/shard_map/pallas_call | solution.py:82
  480.7 1.3 slice_bitcast_fusion
  482.0 51.0 %psum.15 = f32[6,2048]{0,1:T(8,128)} all-reduce(f32[6,2048]{0,1:T(8,128)S(1)} %slice_bitcast_fusion), channel_id=1, replica_groups=mesh['grp'=8,'dev'=16] {'grp'}, use_global_device_ids=true, to_apply=%region_6.7 | all-reduce | flops 12288 | bytes 98304 | tf_op jit(solution)/shard_map/psum | solution.py:168
  533.0 0.7 gather_fusion.11
  533.7 2.0 scatter_custom_fusion.8
  535.7 0.8 copy.151
  536.5 0.7 gather_fusion.8
  537.2 1.7 scatter_custom_fusion.7
  539.0 0.8 copy.150
  539.8 0.7 gather_fusion.7
  540.5 1.4 gather_fusion.6
  541.9 1.2 fusion.9
  543.1 1.5 scatter_custom_fusion.6
  544.6 0.8 copy.149
  545.4 2.3 scatter_custom_fusion.5
  547.7 0.8 copy.148
  (40 shorter events, 3.9 us)
Async XLA Ops:
  5.4 225.2 %copy-start.5 = (s32[256,1]{0,1:T(1,128)}, s32[256,1]{0,1:T(1,128)S(1)}, u32[]{:S(2)}) copy-start(s32[256,1]{0,1:T(1,128)S(1)} %get-tuple-element.40) | copy-start | bytes 3076
  174.7 52.8 %copy-start = (f32[3,1024]{1,0:T(4,128)S(1)}, f32[3,1024]{1,0:T(4,128)}, u32[]{:S(2)}) copy-start(f32[3,1024]{1,0:T(4,128)} %param.8) | copy-start | bytes 36868
  174.7 53.8 %copy-start.1 = (f32[3,1024]{1,0:T(4,128)S(1)}, f32[3,1024]{1,0:T(4,128)}, u32[]{:S(2)}) copy-start(f32[3,1024]{1,0:T(4,128)} %param.9) | copy-start | bytes 36868
  174.7 54.8 %copy-start.2 = (f32[3,1024]{1,0:T(4,128)S(1)}, f32[3,1024]{1,0:T(4,128)}, u32[]{:S(2)}) copy-start(f32[3,1024]{1,0:T(4,128)} %param.10) | copy-start | bytes 36868
  227.5 4.5 copy-start.4
  235.9 5.4 copy-start.3
  239.6 66.0 %copy-start.6 = (s32[256,1]{0,1:T(1,128)S(1)}, s32[256,1]{0,1:T(1,128)}, u32[]{:S(2)}) copy-start(s32[256,1]{0,1:T(1,128)} %get-tuple-element.37) | copy-start | bytes 3076
where the time goes:
time: 547 us; the launch traced here: 548 us
  Pallas kernels  283 us (52%)
  blocking collectives  214 us (39%)
  local copies, waits for them, and re-layouts  40.5 us (7%)
  other arithmetic  10.1 us (2%)
    pallas_call x2, Pallas kernels, pair_terms(): pl.pallas_call(kernel, out_shape=jax.ShapeDtypeStruct((cap, 8), jnp.float...  283 us
    psum x2, blocking collectives, shards(): totals = lax.psum(partial[:, :6].T, 'grp')  101 us
    all_gather x2, blocking collectives, shards(): lax.all_gather(jnp.concatenate([pred_pos, pred_vel], axis=0), 'dev', axis...  84.2 us
    all_gather x2, blocking collectives, shards(): col_targets = lax.all_gather(targets, 'grp', axis=1, tiled=True)  28.9 us

commit v1 on v0

--- a/solution.py
+++ b/solution.py
@@ -159,14 +159,17 @@
         now = (step + 1) * tick_length
         pred_pos, pred_vel = predict(positions, velocities, accelerations, jerks, now - last_time)
         rows = active_rows[step]
-        targets = jnp.concatenate([pred_pos[:, rows], pred_vel[:, rows]], axis=0)
+        targets = jnp.concatenate(
+            [pred_pos[:, rows], pred_vel[:, rows], jnp.zeros((2, slot_cap), jnp.float32)], axis=0
+        ).T
         col_counts = counts[step].reshape(n_grp, n_dev)[:, d_idx]
-        col_targets = lax.all_gather(targets, "grp", axis=1, tiled=True)
-        padded = jnp.concatenate([col_targets, jnp.zeros((2, col_cap), jnp.float32)], axis=0)
+        packed = targets.reshape(slot_cap * 8 // LANES, LANES)
+        col_targets = lax.all_gather(packed, "grp", axis=0, tiled=True).reshape(col_cap, 8)
         src = lax.all_gather(jnp.concatenate([pred_pos, pred_vel], axis=0), "dev", axis=1, tiled=True)
-        partial = pair_terms(col_counts, padded.T, src, mass, soft_sq)
-        totals = lax.psum(partial[:, :6].T, "grp")
-        own = lax.dynamic_slice_in_dim(totals, g_idx * slot_cap, slot_cap, 1)
+        partial = pair_terms(col_counts, col_targets, src, mass, soft_sq)
+        dense = lax.optimization_barrier(partial.reshape(col_cap * 8 // LANES, LANES))
+        totals = lax.optimization_barrier(lax.psum(dense, "grp")).reshape(col_cap, 8)
+        own = lax.dynamic_slice_in_dim(totals, g_idx * slot_cap, slot_cap, 0)[:, :6].T
         own_count = col_counts[g_idx]
         span = now - last_time[rows]
         new_pos, new_vel = correct(

time: 547 us -> 583 us (1.066)
  the two profiles are of different devices: /device:TPU:28 before, /device:TPU:1 now
where the time goes in v1:
time: 583 us; the launch traced here: 574 us
  Pallas kernels  262 us (45%)
  waiting for transfers between devices  175 us (30%)
  blocking collectives  68.6 us (12%)
  local copies, waits for them, and re-layouts  50.1 us (9%)
  between operations  14.5 us (2%)
    pallas_call x2, Pallas kernels, pair_terms(): pl.pallas_call(kernel, out_shape=jax.ShapeDtypeStruct((cap, 8), jnp.float...  262 us
    psum x2, waiting for transfers between devices, shards(): lax.psum(dense, 'grp')  175 us
    all_gather x2, blocking collectives, shards(): lax.all_gather(jnp.concatenate([pred_pos, pred_vel], axis=0), 'dev', axis...  38 us
    all_gather x2, blocking collectives, shards(): lax.all_gather(packed, 'grp', axis=0, tiled=True).reshape(col_cap, 8)  30.6 us
  transfers between devices with their start and end apart: 2, of which 2 were waited for; matrix products, arithmetic and copies ran while one was open for 2% of the time, Pallas kernels for 0%

profile of v1, /device:TPU:1, one launch (start us, length us, event | category | flops | bytes accessed | tf_op | source)
XLA Modules:
  0.0 573.9 jit_solution(6062645356030959223)
XLA Ops:
  7.9 0.8 multiply_add_fusion.3
  9.2 0.8 slice_reduce_fusion
  10.1 0.7 dynamic-slice_reduce_fusion.1.refs_0_
  12.0 2.1 compare_select_fusion
  14.1 0.7 gather_fusion.5
  14.9 0.7 gather_fusion.4
  16.1 15.3 %all_gather.12 = f32[128,128]{1,0:T(8,128)S(1)} all-gather(f32[16,128]{1,0:T(8,128)S(1)} %reshape.184), channel_id=1, replica_groups=mesh['grp'=8,'dev'=16] {'grp'}, dimensions={0}, use_global_device_ids=true | all-gather | bytes 73728 | tf_op jit(solution)/shard_map/all_gather | solution.py:167
  31.4 1.6 reshape.185.refs_1_
  32.9 19.1 %all_gather.13 = f32[6,16384]{1,0:T(8,128)S(1)} all-gather(f32[6,1024]{1,0:T(8,128)S(1)} %pad_maximum_fusion), channel_id=1, replica_groups=mesh['grp'=8,'dev'=16] {'dev'}, dimensions={1}, use_global_device_ids=true | all-gather | bytes 417792 | tf_op jit(solution)/shard_map/all_gather | solution.py:168
  52.0 1.9 broadcast_in_dim.9.refs_2_
  53.9 142.2 %shard_map.102 = f32[2048,8]{1,0:T(8,128)} custom-call(s32[8]{0:T(128)} %dynamic-slice_reduce_fusion.1.refs_0_, f32[2048,8]{1,0:T(8,128)} %reshape.185.refs_1_, f32[6,8,16384]{2,1,0:T(8,128)} %broadcast_in_dim.9.refs_2_), custom_call_target="tpu_custom_call" | custom-call | tf_op jit(solution)/shard_map/pallas_call | solution.py:82
  196.0 2.3 reshape.186
  198.4 1.4 gather_fusion.1
  199.8 1.4 scatter_fusion.1
  202.2 0.7 dynamic-slice_reduce_fusion.refs_0_
  202.9 0.7 gather_fusion.6
  203.7 0.7 gather_fusion.3
  204.5 0.7 gather_fusion.2
  205.3 0.7 gather_fusion
  206.2 1.4 gather_fusion.8
  207.5 71.3 %all-reduce.3.cloned.1.call-done = f32[128,128]{1,0:T(8,128)} async-done(((f32[128,128]{1,0:T(8,128)}), f32[128,128]{1,0:T(8,128)}) %all-reduce.3.cloned.1.call-update) | async-done | bytes 65552 | tf_op jit(solution)/shard_map/psum | solution.py:171
  278.8 1.4 reshape.187
  280.5 1.4 scatter_fusion
  282.0 1.4 scatter_fusion.4
  283.8 1.4 scatter_fusion.3
  285.7 1.4 scatter_fusion.2
  287.7 0.7 gather_fusion.12
  288.6 0.7 gather_fusion.11
  289.7 15.3 %all_gather.14 = f32[128,128]{1,0:T(8,128)S(1)} all-gather(f32[16,128]{1,0:T(8,128)S(1)} %reshape.188), channel_id=1, replica_groups=mesh['grp'=8,'dev'=16] {'grp'}, dimensions={0}, use_global_device_ids=true | all-gather | bytes 73728 | tf_op jit(solution)/shard_map/all_gather | solution.py:167
  305.0 1.6 reshape.189.refs_1_
  306.6 18.9 %all_gather.15 = f32[6,16384]{1,0:T(8,128)S(1)} all-gather(f32[6,1024]{1,0:T(8,128)S(1)} %pad_maximum_fusion.1), channel_id=1, replica_groups=mesh['grp'=8,'dev'=16] {'dev'}, dimensions={1}, use_global_device_ids=true | all-gather | bytes 417792 | tf_op jit(solution)/shard_map/all_gather | solution.py:168
  325.5 1.9 broadcast_in_dim.10.refs_2_
  327.4 119.9 %shard_map.103 = f32[2048,8]{1,0:T(8,128)} custom-call(s32[8]{0:T(128)} %dynamic-slice_reduce_fusion.refs_0_, f32[2048,8]{1,0:T(8,128)} %reshape.189.refs_1_, f32[6,8,16384]{2,1,0:T(8,128)} %broadcast_in_dim.10.refs_2_), custom_call_target="tpu_custom_call" | custom-call | tf_op jit(solution)/shard_map/pallas_call | solution.py:82
  447.3 2.2 reshape.190
  449.6 0.7 gather_fusion.13
  450.3 0.7 gather_fusion.10
  451.0 0.7 gather_fusion.9
  451.8 0.7 gather_fusion.7
  452.8 103.5 %all-reduce.5.cloned.1.call-done = f32[128,128]{1,0:T(8,128)} async-done(((f32[128,128]{1,0:T(8,128)}), f32[128,128]{1,0:T(8,128)}) %all-reduce.5.cloned.1.call-update) | async-done | bytes 65552 | tf_op jit(solution)/shard_map/psum | solution.py:171
  556.3 1.4 reshape.191
  558.0 1.4 scatter_fusion.5
  559.4 0.8 copy.140
  560.3 1.4 scatter_fusion.6
  561.7 0.8 copy.141
  562.6 1.4 scatter_fusion.7
  564.0 0.8 copy.142
  564.9 1.4 scatter_fusion.8
  566.3 0.8 copy.143
  (72 shorter events, 7.7 us)
Async XLA Ops:
  7.2 271.7 %all-reduce.3.cloned.1.call-start = ((), (), s32[]{:S(2)}) async-start(), calls=%async_computation | async-start | bytes 131072 | tf_op jit(solution)/shard_map/psum | solution.py:171
  196.0 5.2 copy-start
  196.0 5.5 copy-start.1
  196.0 5.7 copy-start.2
  196.0 5.9 %copy-start.3 = (f32[3,1024]{1,0:T(4,128)S(1)}, f32[3,1024]{1,0:T(4,128)}, u32[]{:S(2)}) copy-start(f32[3,1024]{1,0:T(4,128)} %param.8) | copy-start | bytes 36868
  198.4 357.9 %all-reduce.5.cloned.1.call-start = ((), (), s32[]{:S(2)}) async-start(), calls=%async_computation.1 | async-start | bytes 131072 | tf_op jit(solution)/shard_map/psum | solution.py:171
Sparse Core Ops, SparseCore 0:
  198.5 80.2 all-reduce.2
  449.7 106.5 all-reduce.4
